TPU v7x, 512 devices: a whole 4x4x16 slice. The times are simulated.
512 devices in a mesh: req: 32 (over x, y, core), ctx: 16 (over z).
Axes of the slice: x: 4, y: 4, z: 16, core: 2. Of those that a mesh axis runs over, the one named last changes fastest.
Arguments:
- queries: bfloat16 [64, 48, 8192], P('req', None, 'ctx'), parts along dimension 0, may hold values from -120 to 120
- key_cache: bfloat16 [64, 2048, 1024], P('req', 'ctx'), parts along dimension 0, may hold values from -5 to 5
- value_cache: bfloat16 [64, 2048, 1024], P('req', 'ctx'), parts along dimension 0, may hold values from -6 to 6
- draft_keys: bfloat16 [64, 48, 1024], P('req', None, 'ctx'), parts along dimension 0, may hold values from -12 to 12
- draft_values: bfloat16 [64, 48, 1024], P('req', None, 'ctx'), parts along dimension 0, may hold values from -6 to 6
- ancestors: int32 [64, 24, 24], P('req'), parts along dimension 0, may hold values from 0 to 1, as said below
- context_length: int32 [32], P('req'), parts along dimension 0, may hold values from 1025 to 2048
Outputs:
- attention: float32 [64, 48, 8192], P('req', None, 'ctx'), parts along dimension 0
There are 32 independent parts, one for each index of `req`. A program takes and returns all parts, laid end to end along the dimension named above; each array names one. Nothing has to cross between parts.
Inputs may be any that keep to these rules, and one draw needn't show every extreme that they name: ancestors[t, n, j] is 1 exactly where node j of tree t is node n itself or one of its ancestors; node 0 is the root of every tree and every other node's parent has a lower number.
All inputs are finite; a program needn't handle non-finite values.
Results may differ from a plain program's by a relative error of at most 0.005.
Values may be sent and summed in bfloat16 or wider, within the bound.
No kernel may reach another device: no remote copies, remote signals or barrier semaphores. Data moves between devices by JAX's collectives and lax.ppermute only.
A program may use at most 64 MiB of HBM per device.

v0:
```python
import math
import jax
import jax.numpy as jnp
from jax import lax
from jax.sharding import PartitionSpec as P

H = 64
KVH = 8
DH = 128
masked_score = -1e30


def sent_together(arrays, axis, dim, along):
    ends, at = ([], 0)
    for a in arrays[:-1]:
        at += a.shape[along]
        ends.append(at)
    both = jnp.concatenate(arrays, axis=along)
    return tuple(jnp.split(lax.all_gather(both, axis, axis=dim, tiled=True), ends, axis=along))


def block_partial(
    query_heads, block_keys, block_values, draft_k, draft_v, cache_keep, draft_keep, score_scale
):
    scores = (
        jnp.einsum("qkjd,pkd->kqjp", query_heads, block_keys, preferred_element_type=jnp.float32)
        * score_scale
    )
    draft_scores = (
        jnp.einsum("qkjd,tkd->kqjt", query_heads, draft_k, preferred_element_type=jnp.float32)
        * score_scale
    )
    scores = jnp.where(cache_keep[None, None, None, :], scores, masked_score)
    draft_scores = jnp.where(draft_keep[None, :, None, :], draft_scores, masked_score)
    top_score = jnp.maximum(jnp.max(scores, -1), jnp.max(draft_scores, -1))
    shift_by = jnp.where(top_score > -1e29, top_score, 0.0)
    cache_weight = jnp.exp(scores - shift_by[..., None])
    draft_weight = jnp.exp(draft_scores - shift_by[..., None])
    total = jnp.sum(cache_weight, -1) + jnp.sum(draft_weight, -1)
    weighted = jnp.einsum(
        "kqjp,pkd->qkjd",
        cache_weight.astype(jnp.bfloat16),
        block_values,
        preferred_element_type=jnp.float32,
    )
    weighted = weighted + jnp.einsum(
        "kqjt,tkd->qkjd",
        draft_weight.astype(jnp.bfloat16),
        draft_v,
        preferred_element_type=jnp.float32,
    )
    top_score = jnp.transpose(top_score, (1, 0, 2))
    total = jnp.transpose(total, (1, 0, 2))
    alive = total > 0.0
    safe_total = jnp.where(alive, total, 1.0)
    output = jnp.where(alive[..., None], weighted / safe_total[..., None], 0.0).astype(jnp.bfloat16)
    lse = jnp.where(alive, top_score + jnp.log(safe_total), masked_score)
    return (lse, output)


def body(queries, key_cache, value_cache, draft_keys, draft_values, ancestors, context_length):
    devices = lax.axis_size("ctx")
    device_index = lax.axis_index("ctx")
    gathered_q, gathered_k, gathered_v = (
        lax.all_gather(queries, "ctx", axis=2, tiled=True),
        *sent_together((draft_keys, draft_values), "ctx", 2, 0),
    )
    layers = gathered_q.shape[0]
    rows = gathered_q.shape[1]
    local_len = key_cache.shape[1]
    trees = ancestors.shape[0]
    group_size = H // KVH
    score_scale = 1.0 / math.sqrt(DH)
    heads_here = H // devices
    tree_keep = (
        jnp.eye(trees, dtype=jnp.int32)[:, None, :, None] * ancestors[:, :, None, :]
    ).reshape(rows, rows) > 0
    draft_keep = jnp.logical_and(tree_keep, device_index == 0)
    cache_keep = (
        device_index * local_len + jnp.arange(local_len, dtype=jnp.int32) < context_length[0]
    )
    results = []
    for layer_index in range(layers):
        query_heads = gathered_q[layer_index].reshape(rows, KVH, group_size, DH)
        lse, output = block_partial(
            query_heads,
            key_cache[layer_index].reshape(local_len, KVH, DH),
            value_cache[layer_index].reshape(local_len, KVH, DH),
            gathered_k[layer_index].reshape(rows, KVH, DH),
            gathered_v[layer_index].reshape(rows, KVH, DH),
            cache_keep,
            draft_keep,
            score_scale,
        )
        lse = lse.reshape(rows, H)
        output = output.reshape(rows, H, DH).astype(jnp.float32)
        lses, outputs = (
            lax.all_to_all(lse[None], "ctx", split_axis=2, concat_axis=0, tiled=True),
            lax.all_to_all(output[None], "ctx", split_axis=2, concat_axis=0, tiled=True),
        )
        overall = jnp.max(lses, 0)
        factor = jnp.exp(lses - overall)
        total_mine = jnp.sum(factor, 0)
        weighted_mine = jnp.sum(factor[..., None] * outputs, 0)
        mine = weighted_mine / total_mine[..., None]
        results.append(mine.reshape(rows, heads_here * DH))
    return jnp.stack(results)


def solution(mesh):
    placed = (
        P("req", None, "ctx"),
        P("req", "ctx", None),
        P("req", "ctx", None),
        P("req", None, "ctx"),
        P("req", None, "ctx"),
        P("req", None, None),
        P("req"),
    )
    return jax.shard_map(
        body, mesh=mesh, in_specs=placed, out_specs=P("req", None, "ctx"), check_vma=False
    )
```

profile of v0, /device:TPU:60, one launch (start us, length us, event | category | flops | bytes accessed | tf_op | source)
XLA Modules:
  0.0 297.8 jit_solution(13309664191307874075)
XLA Ops:
  7.9 0.9 compare_and_fusion
  10.6 1.1 fusion.36
  11.7 0.8 copy.187
  12.6 0.9 copy.189
  15.1 42.9 %all_gather.7 = bf16[4,48,1024]{1,0,2:T(4,128)(2,1)S(1)} all-gather(bf16[4,48,64]{1,0,2:T(4,128)(2,1)S(1)} %pad_maximum_fusion.1), channel_id=1, replica_groups=mesh['req'=32,'ctx'=16] {'ctx'}, dimensions={2}, use_global_device_ids=true | all-gather | bytes 417792 | tf_op jit(solution)/shard_map/all_gather | solution.py:19
  58.0 2.2 fusion.34
  62.5 22.9 %all-gather.2.cloned.1.call-done = bf16[2,48,8192]{2,1,0:T(8,128)(2,1)} async-done(((bf16[2,48,512]{2,1,0:T(8,128)(2,1)}), bf16[2,48,8192]{2,1,0:T(8,128)(2,1)}) %all-gather.2.cloned.1.call-update) | async-done | bytes 1572880 | tf_op jit(solution)/shard_map/all_gather | solution.py:65
  85.5 1.5 slice_bitcast_fusion.1
  87.3 2.2 fusion.40
  89.7 1.6 fusion.39
  91.4 2.7 fusion.11
  94.2 0.9 fusion.9
  95.2 1.8 fusion.18
  99.9 8.3 %all-to-all-start = ((f32[16,1,192]{2,1,0:T(1,128)}), f32[16,1,192]{2,1,0:T(1,128)S(1)}, u32[]{:S(2)}, u32[]{:S(2)}) async-start(f32[16,1,192]{2,1,0:T(1,128)} %reshape.145), calls=%async_computation | async-start | bytes 32768 | tf_op jit(solution)/shard_map/all_to_all | solution.py:98
  108.1 2.2 fusion.38
  111.2 2.7 fusion.15
  114.0 0.9 fusion.13
  115.8 1.3 copy.140
  119.4 11.3 %all-to-all-start.2 = ((f32[16,1,192]{2,1,0:T(1,128)}), f32[16,1,192]{2,1,0:T(1,128)S(1)}, u32[]{:S(2)}, u32[]{:S(2)}) async-start(f32[16,1,192]{2,1,0:T(1,128)} %reshape.143), calls=%async_computation.2 | async-start | bytes 32768 | tf_op jit(solution)/shard_map/all_to_all | solution.py:98
  130.7 2.3 fusion.6
  133.2 2.1 copy.142
  135.3 6.8 %all-to-all-done.2 = f32[16,1,192]{2,1,0:T(1,128)S(1)} async-done(((f32[16,1,192]{2,1,0:T(1,128)}), f32[16,1,192]{2,1,0:T(1,128)S(1)}, u32[]{:S(2)}, u32[]{:S(2)}) %all-to-all-start.2) | async-done | bytes 12320 | tf_op jit(solution)/shard_map/all_to_all | solution.py:98
  142.7 5.2 %all-to-all-start.1 = ((f32[1,48,64,128]{3,1,0,2:T(8,128)}), f32[1,48,64,128]{3,1,0,2:T(8,128)S(1)}, u32[]{:S(2)}, u32[]{:S(2)}) async-start(f32[1,48,64,128]{3,1,0,2:T(8,128)} %copy.142), calls=%async_computation.1 | async-start | bytes 3145728 | tf_op jit(solution)/shard_map/all_to_all | solution.py:99
  147.9 1.8 copy.190
  149.7 1.2 copy.157
  150.9 2.4 copy.159
  153.3 1.6 fusion.16
  155.0 1.5 fusion.7
  156.7 2.1 copy.161
  158.8 49.8 %all-to-all-done.1 = f32[1,48,64,128]{3,1,0,2:T(8,128)S(1)} async-done(((f32[1,48,64,128]{3,1,0,2:T(8,128)}), f32[1,48,64,128]{3,1,0,2:T(8,128)S(1)}, u32[]{:S(2)}, u32[]{:S(2)}) %all-to-all-start.1) | async-done | bytes 1572896 | tf_op jit(solution)/shard_map/all_to_all | solution.py:99
  208.6 10.4 %all-to-all-start.3 = ((f32[1,48,64,128]{3,1,0,2:T(8,128)}), f32[1,48,64,128]{3,1,0,2:T(8,128)S(1)}, u32[]{:S(2)}, u32[]{:S(2)}) async-start(f32[1,48,64,128]{3,1,0,2:T(8,128)} %copy.161), calls=%async_computation.3 | async-start | bytes 3145728 | tf_op jit(solution)/shard_map/all_to_all | solution.py:99
  221.5 68.1 %all-to-all-done.3 = f32[1,48,64,128]{3,1,0,2:T(8,128)S(1)} async-done(((f32[1,48,64,128]{3,1,0,2:T(8,128)}), f32[1,48,64,128]{3,1,0,2:T(8,128)S(1)}, u32[]{:S(2)}, u32[]{:S(2)}) %all-to-all-start.3) | async-done | bytes 1572896 | tf_op jit(solution)/shard_map/all_to_all | solution.py:99
  (92 shorter events, 18.9 us)
Async XLA Ops:
  6.5 6.9 %copy-start.4 = (bf16[2,128,1024]{2,1,0:T(8,128)(2,1)S(1)}, bf16[2,128,1024]{2,1,0:T(8,128)(2,1)}, u32[]{:S(2)}) copy-start(bf16[2,128,1024]{2,1,0:T(8,128)(2,1)} %param.9) | copy-start | bytes 1572868
  6.5 78.9 %all-gather.2.cloned.1.call-start = ((), (), s32[]{:S(2)}) async-start(), calls=%async_computation.4 | async-start | bytes 1671168 | tf_op jit(solution)/shard_map/all_gather | solution.py:65
  9.0 78.4 %copy-start.11 = (pred[48,48]{0,1:T(8,128)(4,1)}, pred[48,48]{0,1:T(8,128)(4,1)S(1)}, u32[]{:S(2)}) copy-start(pred[48,48]{0,1:T(8,128)(4,1)S(1)} %copy.125) | copy-start | bytes 6916
  62.5 27.2 %copy-start.15 = (pred[128]{0:T(512)(128)(4,1)}, pred[128]{0:T(512)(128)(4,1)S(1)}, u32[]{:S(2)}) copy-start(pred[128]{0:T(512)(128)(4,1)S(1)} %add_compare_fusion) | copy-start | bytes 388
  94.1 1.1 copy-start.2
  96.9 11.2 %copy-start.5 = (bf16[6,8,8,128]{3,2,1,0:T(8,128)(2,1)S(1)}, bf16[6,8,8,128]{3,2,1,0:T(8,128)(2,1)}, u32[]{:S(2)}) copy-start(bf16[6,8,8,128]{3,2,1,0:T(8,128)(2,1)} %copy.195) | copy-start | bytes 294916
  96.9 11.2 %copy-start.12 = (pred[48,48]{0,1:T(8,128)(4,1)S(1)}, pred[48,48]{0,1:T(8,128)(4,1)}, u32[]{:S(2)}) copy-start(pred[48,48]{0,1:T(8,128)(4,1)} %copy-done.11) | copy-start | bytes 6916
  97.7 12.8 %copy-start.1 = (bf16[1,128,1024]{1,2,0:T(8,128)(2,1)S(1)}, bf16[1,128,1024]{1,2,0:T(8,128)(2,1)}, u32[]{:S(2)}) copy-start(bf16[1,128,1024]{1,2,0:T(8,128)(2,1)} %copy.189) | copy-start | bytes 786436
  97.7 12.8 %copy-start.16 = (pred[128]{0:T(512)(128)(4,1)S(1)}, pred[128]{0:T(512)(128)(4,1)}, u32[]{:S(2)}) copy-start(pred[128]{0:T(512)(128)(4,1)} %copy-done.15) | copy-start | bytes 388
  99.9 19.5 %all-to-all-start = ((f32[16,1,192]{2,1,0:T(1,128)}), f32[16,1,192]{2,1,0:T(1,128)S(1)}, u32[]{:S(2)}, u32[]{:S(2)}) async-start(f32[16,1,192]{2,1,0:T(1,128)} %reshape.145), calls=%async_computation | async-start | bytes 32768 | tf_op jit(solution)/shard_map/all_to_all | solution.py:98
  114.0 1.7 copy-start
  115.0 15.7 %copy-start.6 = (f32[48,8,8]{2,0,1:T(8,128)S(1)}, f32[48,8,8]{2,0,1:T(8,128)}, u32[]{:S(2)}) copy-start(f32[48,8,8]{2,0,1:T(8,128)} %get-tuple-element.8) | copy-start | bytes 36868
  115.7 14.9 %copy-start.8 = (bf16[6,8,8,128]{3,2,1,0:T(8,128)(2,1)S(1)}, bf16[6,8,8,128]{3,2,1,0:T(8,128)(2,1)}, u32[]{:S(2)}) copy-start(bf16[6,8,8,128]{3,2,1,0:T(8,128)(2,1)} %copy.193) | copy-start | bytes 294916
  115.8 14.9 %copy-start.13 = (pred[48,8,8]{2,0,1:T(8,128)(4,1)S(1)}, pred[48,8,8]{2,0,1:T(8,128)(4,1)}, u32[]{:S(2)}) copy-start(pred[48,8,8]{2,0,1:T(8,128)(4,1)} %get-tuple-element.9) | copy-start | bytes 9220
  119.4 22.7 %all-to-all-start.2 = ((f32[16,1,192]{2,1,0:T(1,128)}), f32[16,1,192]{2,1,0:T(1,128)S(1)}, u32[]{:S(2)}, u32[]{:S(2)}) async-start(f32[16,1,192]{2,1,0:T(1,128)} %reshape.143), calls=%async_computation.2 | async-start | bytes 32768 | tf_op jit(solution)/shard_map/all_to_all | solution.py:98
  142.1 0.6 copy-start.9
  142.7 65.9 %all-to-all-start.1 = ((f32[1,48,64,128]{3,1,0,2:T(8,128)}), f32[1,48,64,128]{3,1,0,2:T(8,128)S(1)}, u32[]{:S(2)}, u32[]{:S(2)}) async-start(f32[1,48,64,128]{3,1,0,2:T(8,128)} %copy.142), calls=%async_computation.1 | async-start | bytes 3145728 | tf_op jit(solution)/shard_map/all_to_all | solution.py:99
  153.3 1.6 copy-start.3
  153.3 1.6 copy-start.7
  153.3 1.7 copy-start.14
  158.8 61.0 %copy-start.10 = (f32[16,1,192]{2,1,0:T(1,128)S(1)}, f32[16,1,192]{2,1,0:T(1,128)}, u32[]{:S(2)}) copy-start(f32[16,1,192]{2,1,0:T(1,128)} %copy-done.9) | copy-start | bytes 36868
  208.6 80.9 %all-to-all-start.3 = ((f32[1,48,64,128]{3,1,0,2:T(8,128)}), f32[1,48,64,128]{3,1,0,2:T(8,128)S(1)}, u32[]{:S(2)}, u32[]{:S(2)}) async-start(f32[1,48,64,128]{3,1,0,2:T(8,128)} %copy.161), calls=%async_computation.3 | async-start | bytes 3145728 | tf_op jit(solution)/shard_map/all_to_all | solution.py:99
Sparse Core Ops, SparseCore 0:
  9.4 75.9 all-gather.1
where the time goes:
time: 299 us; the launch traced here: 298 us
  waiting for transfers between devices  149 us (50%)
  blocking collectives  42.9 us (14%)
  starting transfers between devices  35.1 us (12%)
  local copies, waits for them, and re-layouts  27.5 us (9%)
  other arithmetic  14.7 us (5%)
  between operations  14.5 us (5%)
  matrix products  13.9 us (5%)
    all_to_all x2, waiting for transfers between devices, body(): lax.all_to_all(output[None], 'ctx', split_axis=2, concat_axis=0, tiled=True)  118 us
    all_gather x1, blocking collectives, sent_together(): lax.all_gather(both, axis, axis=dim, tiled=True)  42.9 us
    all_gather x1, waiting for transfers between devices, body(): lax.all_gather(queries, 'ctx', axis=2, tiled=True)  22.9 us
    all_to_all x2, starting transfers between devices, body(): lax.all_to_all(lse[None], 'ctx', split_axis=2, concat_axis=0, tiled=True)  19.5 us
    all_to_all x2, starting transfers between devices, body(): lax.all_to_all(output[None], 'ctx', split_axis=2, concat_axis=0, tiled=True)  15.6 us
    unnamed x52, local copies, waits for them, and re-layouts  12 us
    all_to_all x2, waiting for transfers between devices, body(): lax.all_to_all(lse[None], 'ctx', split_axis=2, concat_axis=0, tiled=True)  7.55 us
    reduce_sum x4, other arithmetic, block_partial(): total = jnp.sum(cache_weight, -1) + jnp.sum(draft_weight, -1)  7.23 us
  transfers between devices with their start and end apart: 5, of which 5 were waited for; matrix products, arithmetic and copies ran while one was open for 13% of the time, Pallas kernels for 0%

commit v1 on v0

--- a/solution.py
+++ b/solution.py
@@ -8,6 +8,15 @@
 KVH = 8
 DH = 128
 masked_score = -1e30
+panel_write = lambda piece_in: jnp.concatenate(
+    lax.all_to_all(
+        jnp.stack([piece_in] * lax.psum(1, axis_name="ctx")),
+        axis_name="ctx",
+        split_axis=0,
+        concat_axis=0,
+    ),
+    axis=2,
+)
 
 
 def sent_together(arrays, axis, dim, along):
@@ -62,7 +71,7 @@
     devices = lax.axis_size("ctx")
     device_index = lax.axis_index("ctx")
     gathered_q, gathered_k, gathered_v = (
-        lax.all_gather(queries, "ctx", axis=2, tiled=True),
+        panel_write(queries),
         *sent_together((draft_keys, draft_values), "ctx", 2, 0),
     )
     layers = gathered_q.shape[0]

time: 299 us -> 336 us (1.12)
  the two profiles are of different devices: /device:TPU:60 before, /device:TPU:8 now
where the time goes in v1:
time: 336 us
  waiting for transfers between devices  135 us (40%)
  blocking collectives  95.9 us (29%)
  starting transfers between devices  47.9 us (14%)
  local copies, waits for them, and re-layouts  27.3 us (8%)
  other arithmetic  14 us (4%)
  matrix products  13.9 us (4%)
    all_to_all x2, waiting for transfers between devices, body(): lax.all_to_all(output[None], 'ctx', split_axis=2, concat_axis=0, tiled=True)  125 us
    all_gather x1, blocking collectives, sent_together(): lax.all_gather(both, axis, axis=dim, tiled=True)  95.9 us
    all_to_all x2, starting transfers between devices, body(): lax.all_to_all(lse[None], 'ctx', split_axis=2, concat_axis=0, tiled=True)  19.8 us
    all_to_all x1, starting transfers between devices, lax.all_to_all(jnp.stack([piece_in] * lax.psum(1, axis_name='ctx')), axis...  15.3 us
    all_to_all x2, starting transfers between devices, body(): lax.all_to_all(output[None], 'ctx', split_axis=2, concat_axis=0, tiled=True)  12.8 us
    all_to_all x2, waiting for transfers between devices, body(): lax.all_to_all(lse[None], 'ctx', split_axis=2, concat_axis=0, tiled=True)  9.87 us
    unnamed x57, local copies, waits for them, and re-layouts  8.75 us
    reduce_sum x4, other arithmetic, block_partial(): total = jnp.sum(cache_weight, -1) + jnp.sum(draft_weight, -1)  7.23 us
  transfers between devices with their start and end apart: 5, of which 4 were waited for; matrix products, arithmetic and copies ran while one was open for 11% of the time, Pallas kernels for 0%

profile of v1, /device:TPU:8, one launch (start us, length us, event | category | flops | bytes accessed | tf_op | source)
XLA Modules:
  0.0 335.6 jit_solution(12616410748228676662)
XLA Ops:
  0.0 2.2 stack.4
  2.2 15.3 %all-to-all-start = ((bf16[16,2,48,512]{3,2,1,0:T(8,128)(2,1)}), bf16[16,2,48,512]{3,2,1,0:T(8,128)(2,1)S(1)}, u32[]{:S(2)}, u32[]{:S(2)}) async-start(bf16[16,2,48,512]{3,2,1,0:T(8,128)(2,1)} %stack.4), calls=%async_computation | async-start | bytes 3145728 | tf_op jit(solution)/shard_map/all_to_all | solution.py:12
  18.9 0.9 copy.193
  19.8 0.8 copy.195
  21.4 0.8 copy.196
  22.3 95.9 %all_gather.3 = bf16[4,48,1024]{1,0,2:T(4,128)(2,1)S(1)} all-gather(bf16[4,48,64]{1,0,2:T(4,128)(2,1)S(1)} %pad_maximum_fusion.1), channel_id=1, replica_groups=mesh['req'=32,'ctx'=16] {'ctx'}, dimensions={2}, use_global_device_ids=true | all-gather | bytes 417792 | tf_op jit(solution)/shard_map/all_gather | solution.py:28
  118.2 2.2 fusion.35
  124.7 2.2 fusion.39
  127.1 1.6 fusion.38
  128.8 2.7 fusion.15
  131.6 0.9 fusion.13
  132.5 1.8 fusion.16
  137.2 9.7 %all-to-all-start.3 = ((f32[16,1,192]{2,1,0:T(1,128)}), f32[16,1,192]{2,1,0:T(1,128)S(1)}, u32[]{:S(2)}, u32[]{:S(2)}) async-start(f32[16,1,192]{2,1,0:T(1,128)} %reshape.154), calls=%async_computation.3 | async-start | bytes 32768 | tf_op jit(solution)/shard_map/all_to_all | solution.py:107
  147.0 2.2 fusion.41
  150.1 2.7 fusion.11
  152.9 0.9 fusion.9
  154.7 1.3 copy.165
  157.5 2.0 all-to-all-done.3
  159.5 10.0 %all-to-all-start.1 = ((f32[16,1,192]{2,1,0:T(1,128)}), f32[16,1,192]{2,1,0:T(1,128)S(1)}, u32[]{:S(2)}, u32[]{:S(2)}) async-start(f32[16,1,192]{2,1,0:T(1,128)} %reshape.156), calls=%async_computation.1 | async-start | bytes 32768 | tf_op jit(solution)/shard_map/all_to_all | solution.py:107
  169.6 2.3 fusion.7
  172.1 2.1 copy.167
  174.2 7.9 %all-to-all-done.1 = f32[16,1,192]{2,1,0:T(1,128)S(1)} async-done(((f32[16,1,192]{2,1,0:T(1,128)}), f32[16,1,192]{2,1,0:T(1,128)S(1)}, u32[]{:S(2)}, u32[]{:S(2)}) %all-to-all-start.1) | async-done | bytes 12320 | tf_op jit(solution)/shard_map/all_to_all | solution.py:107
  182.6 4.2 %all-to-all-start.4 = ((f32[1,48,64,128]{3,1,0,2:T(8,128)}), f32[1,48,64,128]{3,1,0,2:T(8,128)S(1)}, u32[]{:S(2)}, u32[]{:S(2)}) async-start(f32[1,48,64,128]{3,1,0,2:T(8,128)} %copy.167), calls=%async_computation.4 | async-start | bytes 3145728 | tf_op jit(solution)/shard_map/all_to_all | solution.py:108
  186.8 1.8 copy.194
  188.6 1.2 copy.143
  189.8 2.4 copy.145
  192.2 1.6 fusion.18
  193.9 1.5 fusion.6
  195.6 2.1 copy.147
  197.7 54.5 %all-to-all-done.4 = f32[1,48,64,128]{3,1,0,2:T(8,128)S(1)} async-done(((f32[1,48,64,128]{3,1,0,2:T(8,128)}), f32[1,48,64,128]{3,1,0,2:T(8,128)S(1)}, u32[]{:S(2)}, u32[]{:S(2)}) %all-to-all-start.4) | async-done | bytes 1572896 | tf_op jit(solution)/shard_map/all_to_all | solution.py:108
  252.2 8.7 %all-to-all-start.2 = ((f32[1,48,64,128]{3,1,0,2:T(8,128)}), f32[1,48,64,128]{3,1,0,2:T(8,128)S(1)}, u32[]{:S(2)}, u32[]{:S(2)}) async-start(f32[1,48,64,128]{3,1,0,2:T(8,128)} %copy.147), calls=%async_computation.2 | async-start | bytes 3145728 | tf_op jit(solution)/shard_map/all_to_all | solution.py:108
  263.4 70.8 %all-to-all-done.2 = f32[1,48,64,128]{3,1,0,2:T(8,128)S(1)} async-done(((f32[1,48,64,128]{3,1,0,2:T(8,128)}), f32[1,48,64,128]{3,1,0,2:T(8,128)S(1)}, u32[]{:S(2)}, u32[]{:S(2)}) %all-to-all-start.2) | async-done | bytes 1572896 | tf_op jit(solution)/shard_map/all_to_all | solution.py:108
  (102 shorter events, 16.9 us)
Async XLA Ops:
  2.2 16.1 %copy-start.18 = (s32[2,24,24]{2,1,0:T(8,128)S(1)}, s32[2,24,24]{2,1,0:T(8,128)}, u32[]{:S(2)}) copy-start(s32[2,24,24]{2,1,0:T(8,128)} %param.12) | copy-start | bytes 13828
  2.2 16.4 %copy-start.16 = (bf16[2,48,64]{2,1,0:T(8,128)(2,1)S(1)}, bf16[2,48,64]{2,1,0:T(8,128)(2,1)}, u32[]{:S(2)}) copy-start(bf16[2,48,64]{2,1,0:T(8,128)(2,1)} %param.10) | copy-start | bytes 36868
  2.2 16.5 %copy-start.17 = (bf16[2,48,64]{2,1,0:T(8,128)(2,1)S(1)}, bf16[2,48,64]{2,1,0:T(8,128)(2,1)}, u32[]{:S(2)}) copy-start(bf16[2,48,64]{2,1,0:T(8,128)(2,1)} %param.11) | copy-start | bytes 36868
  2.2 16.6 %copy-start.4 = (bf16[2,128,1024]{2,1,0:T(8,128)(2,1)S(1)}, bf16[2,128,1024]{2,1,0:T(8,128)(2,1)}, u32[]{:S(2)}) copy-start(bf16[2,128,1024]{2,1,0:T(8,128)(2,1)} %param.8) | copy-start | bytes 1572868
  2.2 120.5 %all-to-all-start = ((bf16[16,2,48,512]{3,2,1,0:T(8,128)(2,1)}), bf16[16,2,48,512]{3,2,1,0:T(8,128)(2,1)S(1)}, u32[]{:S(2)}, u32[]{:S(2)}) async-start(bf16[16,2,48,512]{3,2,1,0:T(8,128)(2,1)} %stack.4), calls=%async_computation | async-start | bytes 3145728 | tf_op jit(solution)/shard_map/all_to_all | solution.py:12
  17.6 3.0 copy-start.5
  18.6 106.1 %copy-start.12 = (pred[48,48]{0,1:T(8,128)(4,1)}, pred[48,48]{0,1:T(8,128)(4,1)S(1)}, u32[]{:S(2)}) copy-start(pred[48,48]{0,1:T(8,128)(4,1)S(1)} %copy.130) | copy-start | bytes 6916
  122.7 4.3 %copy-start.19 = (pred[128]{0:T(512)(128)(4,1)}, pred[128]{0:T(512)(128)(4,1)S(1)}, u32[]{:S(2)}) copy-start(pred[128]{0:T(512)(128)(4,1)S(1)} %add_compare_fusion) | copy-start | bytes 388
  131.5 1.1 copy-start.2
  134.3 12.7 %copy-start.6 = (bf16[6,8,8,128]{3,2,1,0:T(8,128)(2,1)S(1)}, bf16[6,8,8,128]{3,2,1,0:T(8,128)(2,1)}, u32[]{:S(2)}) copy-start(bf16[6,8,8,128]{3,2,1,0:T(8,128)(2,1)} %copy.197) | copy-start | bytes 294916
  134.3 12.7 %copy-start.13 = (pred[48,48]{0,1:T(8,128)(4,1)S(1)}, pred[48,48]{0,1:T(8,128)(4,1)}, u32[]{:S(2)}) copy-start(pred[48,48]{0,1:T(8,128)(4,1)} %copy-done.12) | copy-start | bytes 6916
  135.1 14.3 %copy-start.1 = (bf16[1,128,1024]{1,2,0:T(8,128)(2,1)S(1)}, bf16[1,128,1024]{1,2,0:T(8,128)(2,1)}, u32[]{:S(2)}) copy-start(bf16[1,128,1024]{1,2,0:T(8,128)(2,1)} %copy.193) | copy-start | bytes 786436
  135.1 14.3 %copy-start.20 = (pred[128]{0:T(512)(128)(4,1)S(1)}, pred[128]{0:T(512)(128)(4,1)}, u32[]{:S(2)}) copy-start(pred[128]{0:T(512)(128)(4,1)} %copy-done.19) | copy-start | bytes 388
  137.2 22.3 %all-to-all-start.3 = ((f32[16,1,192]{2,1,0:T(1,128)}), f32[16,1,192]{2,1,0:T(1,128)S(1)}, u32[]{:S(2)}, u32[]{:S(2)}) async-start(f32[16,1,192]{2,1,0:T(1,128)} %reshape.154), calls=%async_computation.3 | async-start | bytes 32768 | tf_op jit(solution)/shard_map/all_to_all | solution.py:107
  152.9 1.7 copy-start
  153.8 15.7 %copy-start.7 = (f32[48,8,8]{2,0,1:T(8,128)S(1)}, f32[48,8,8]{2,0,1:T(8,128)}, u32[]{:S(2)}) copy-start(f32[48,8,8]{2,0,1:T(8,128)} %get-tuple-element.13) | copy-start | bytes 36868
  154.6 14.9 %copy-start.9 = (bf16[6,8,8,128]{3,2,1,0:T(8,128)(2,1)S(1)}, bf16[6,8,8,128]{3,2,1,0:T(8,128)(2,1)}, u32[]{:S(2)}) copy-start(bf16[6,8,8,128]{3,2,1,0:T(8,128)(2,1)} %copy.200) | copy-start | bytes 294916
  154.6 14.9 %copy-start.14 = (pred[48,8,8]{2,0,1:T(8,128)(4,1)S(1)}, pred[48,8,8]{2,0,1:T(8,128)(4,1)}, u32[]{:S(2)}) copy-start(pred[48,8,8]{2,0,1:T(8,128)(4,1)} %get-tuple-element.14) | copy-start | bytes 9220
  159.5 22.5 %all-to-all-start.1 = ((f32[16,1,192]{2,1,0:T(1,128)}), f32[16,1,192]{2,1,0:T(1,128)S(1)}, u32[]{:S(2)}, u32[]{:S(2)}) async-start(f32[16,1,192]{2,1,0:T(1,128)} %reshape.156), calls=%async_computation.1 | async-start | bytes 32768 | tf_op jit(solution)/shard_map/all_to_all | solution.py:107
  182.0 0.6 copy-start.10
  182.6 69.6 %all-to-all-start.4 = ((f32[1,48,64,128]{3,1,0,2:T(8,128)}), f32[1,48,64,128]{3,1,0,2:T(8,128)S(1)}, u32[]{:S(2)}, u32[]{:S(2)}) async-start(f32[1,48,64,128]{3,1,0,2:T(8,128)} %copy.167), calls=%async_computation.4 | async-start | bytes 3145728 | tf_op jit(solution)/shard_map/all_to_all | solution.py:108
  192.2 1.6 copy-start.3
  192.2 1.6 copy-start.8
  192.2 1.7 copy-start.15
  197.7 64.1 %copy-start.11 = (f32[16,1,192]{2,1,0:T(1,128)S(1)}, f32[16,1,192]{2,1,0:T(1,128)}, u32[]{:S(2)}) copy-start(f32[16,1,192]{2,1,0:T(1,128)} %copy-done.10) | copy-start | bytes 36868
  252.2 82.0 %all-to-all-start.2 = ((f32[1,48,64,128]{3,1,0,2:T(8,128)}), f32[1,48,64,128]{3,1,0,2:T(8,128)S(1)}, u32[]{:S(2)}, u32[]{:S(2)}) async-start(f32[1,48,64,128]{3,1,0,2:T(8,128)} %copy.147), calls=%async_computation.2 | async-start | bytes 3145728 | tf_op jit(solution)/shard_map/all_to_all | solution.py:108
